TPU v7x, 512 devices: a whole 4x8x8 slice. The times are simulated.
512 devices in a mesh: req: 4 (over x), exp: 8 (over z), shard: 16 (over y, core).
Axes of the slice: x: 4, y: 8, z: 8, core: 2. Of those that a mesh axis runs over, the one named last changes fastest.
Arguments:
- query_stretch: bfloat16 [8, 128, 2304], P('req', 'exp'), may hold values from -8 to 8
- resid_stretch: bfloat16 [8, 128, 2304], P('req', 'exp'), may hold values from -30 to 30
- route_ids: int32 [8, 128, 2], P('req', 'exp'), may hold values from 0 to 7, all different within a row; in each aligned block of 16 rows (0 to 15, 16 to 31, ..., all dimensions but the last counted through in order) at most 6 rows name the same one
- route_probs: bfloat16 [8, 128, 2], P('req', 'exp'), may hold values from 0.19921875 to 1
- request_order: int32 [8], replicated, may hold values from 0 to 7, each once
- prior_pages: int32 [4, 2], P('req'), may hold values from 63 to 189, as said below
- page_order: int32 [4, 256], P('req'), may hold values from 0 to 255, each once within a row
- key_pool: bfloat16 [4, 256, 64, 2304], P('req', ('exp', 'shard')), may hold values from -8 to 8
- value_pool: bfloat16 [4, 256, 64, 2304], P('req', ('exp', 'shard')), may hold values from -6 to 6
- norm_gain: float32 [2304], replicated, may hold values from 0.4 to 2.5
- out_proj: bfloat16 [2304, 2304], P('shard'), may hold values from -0.125 to 0.125
- gate_up: bfloat16 [8, 2, 2880, 2304], P('exp', None, 'shard'), may hold values from -0.125 to 0.125
- down_proj: bfloat16 [8, 2880, 2304], P('exp', 'shard'), may hold values from -0.109375 to 0.109375
Outputs:
- mixed_out: bfloat16 [8, 128, 2304], P('req', 'exp')
Inputs may be any that keep to these rules, and one draw needn't show every extreme that they name: `route_ids`: each row names 2 different experts. In each aligned block of 16 rows (one request's tokens b * 16 to (b + 1) * 16 - 1) no expert is named by more than 6 rows, a bound that some block reaches. `request_order`: A permutation of the requests. `prior_pages`: in each group the 2 counts sum to 252, so that the pool is full; one member of every group has exactly 189. `page_order`: each row is a permutation of the group's pool pages.
All inputs are finite; a program needn't handle non-finite values.
Results may differ from a plain program's by a relative error of at most 0.02.
Values may be sent and summed in bfloat16 or wider, within the bound.
No kernel may reach another device: no remote copies, remote signals or barrier semaphores. Data moves between devices by JAX's collectives and lax.ppermute only.
A program may use at most 64 MiB of HBM per device.

v0:
```python
import math
import jax
import jax.numpy as jnp
from jax import lax
from jax.sharding import PartitionSpec as P

H = 36
NEG_FILL = -1e30
EPSILON = 1e-06


def expert_rows(received, gate_up, down_proj):
    width = received.shape[-1]
    flat_rows = received.reshape(-1, width)
    both = lax.dot_general(
        flat_rows, gate_up[0], (((1,), (2,)), ((), ())), preferred_element_type=jnp.float32
    )
    active = (jax.nn.silu(both[:, 0]) * both[:, 1]).astype(jnp.bfloat16)
    partial_out = jnp.dot(active, down_proj[0], preferred_element_type=jnp.float32)
    return partial_out.reshape(received.shape)


def on_device(
    query_stretch,
    resid_stretch,
    route_ids,
    route_probs,
    request_order,
    prior_pages,
    page_order,
    key_pool,
    value_pool,
    norm_gain,
    out_proj,
    gate_up,
    down_proj,
):
    members = prior_pages.shape[1]
    tokens_here = query_stretch.shape[1]
    width = query_stretch.shape[2]
    head_size = width // H
    group_index = lax.axis_index("req")
    exp_index = lax.axis_index("exp")
    shard_index = lax.axis_index("shard")
    shard_count = lax.axis_size("shard")
    experts_count = lax.axis_size("exp")
    all_query, all_resid, all_ids, all_probs = (
        lax.all_gather(query_stretch, "req", axis=0, tiled=True),
        lax.all_gather(resid_stretch, "req", axis=0, tiled=True),
        lax.all_gather(route_ids, "req", axis=0, tiled=True),
        lax.all_gather(route_probs, "req", axis=0, tiled=True),
    )
    served = lax.dynamic_slice_in_dim(request_order, group_index * members, members)
    served_query = jnp.take(all_query, served, axis=0)
    served_resid = jnp.take(all_resid, served, axis=0)
    served_ids = jnp.take(all_ids, served, axis=0)
    served_probs = jnp.take(all_probs, served, axis=0)
    group_query = lax.all_gather(served_query, "exp", axis=1, tiled=True)
    stretch_len = group_query.shape[1]
    pages_here = key_pool.shape[1]
    page_size = key_pool.shape[2]
    device_index = exp_index * shard_count + shard_index
    physical = device_index * pages_here + jnp.arange(pages_here, dtype=jnp.int32)
    page_row = page_order[0]
    pool_size = page_row.shape[0]
    matched = page_row[None, :] == physical[:, None]
    located = jnp.sum(
        jnp.where(matched, jnp.arange(pool_size, dtype=jnp.int32)[None, :], 0), axis=1
    )
    prior_row = prior_pages[0]
    page_counts = prior_row + stretch_len // page_size
    page_ends = jnp.cumsum(page_counts)
    page_starts = page_ends - page_counts
    owner_slot = jnp.sum((located[:, None] >= page_ends[None, :]).astype(jnp.int32), axis=1)
    owner_hot = owner_slot[:, None] == jnp.arange(members, dtype=jnp.int32)[None, :]
    logical = located - jnp.sum(jnp.where(owner_hot, page_starts[None, :], 0), axis=1)
    prior_here = jnp.sum(jnp.where(owner_hot, prior_row[None, :], 0), axis=1)
    key_place = logical[:, None] * page_size + jnp.arange(page_size, dtype=jnp.int32)[None, :]
    query_place = (
        prior_here[:, None] * page_size + jnp.arange(stretch_len, dtype=jnp.int32)[None, :]
    )
    visible = key_place[:, None, :] <= query_place[:, :, None]
    page_query = jnp.take(group_query, owner_slot, axis=0).reshape(
        pages_here, stretch_len, H, head_size
    )
    key_rows = key_pool[0].reshape(pages_here, page_size, H, head_size)
    value_rows = value_pool[0].reshape(pages_here, page_size, H, head_size)
    scores = jnp.einsum(
        "pqhd,pkhd->phqk", page_query, key_rows, preferred_element_type=jnp.float32
    ) * (1.0 / math.sqrt(head_size))
    scores = jnp.where(visible[:, None, :, :], scores, NEG_FILL)
    page_peak = jnp.max(scores, axis=3)
    local_peak = jnp.max(
        jnp.where(owner_hot[:, :, None, None], page_peak[:, None], NEG_FILL), axis=0
    )
    row_peak = lax.pmax(local_peak, ("exp", "shard"))
    peak_here = jnp.take(row_peak, owner_slot, axis=0)
    weights_bf = jnp.where(
        visible[:, None, :, :], jnp.exp(scores - peak_here[..., None]), 0.0
    ).astype(jnp.bfloat16)
    page_totals = jnp.sum(weights_bf, axis=3, dtype=jnp.float32)
    page_context = jnp.einsum(
        "phqk,pkhd->pqhd", weights_bf, value_rows, preferred_element_type=jnp.float32
    )
    page_context = page_context.reshape(pages_here, stretch_len, width)
    context = jnp.sum(jnp.where(owner_hot[:, :, None, None], page_context[:, None], 0.0), axis=0)
    totals = jnp.sum(jnp.where(owner_hot[:, :, None, None], page_totals[:, None], 0.0), axis=0)
    context_all, totals_all = lax.psum((context, totals), ("exp", "shard"))
    context_mine = lax.dynamic_slice_in_dim(context_all, exp_index * tokens_here, tokens_here, 1)
    totals_mine = lax.dynamic_slice_in_dim(totals_all, exp_index * tokens_here, tokens_here, 2)
    per_head = context_mine.reshape(members, tokens_here, H, head_size)
    attended = (
        (per_head / jnp.transpose(totals_mine, (0, 2, 1))[..., None])
        .reshape(members, tokens_here, width)
        .astype(jnp.bfloat16)
    )
    projected_part = lax.dot_general(
        attended, out_proj, (((2,), (1,)), ((), ())), preferred_element_type=jnp.float32
    ).astype(jnp.bfloat16)
    projected = lax.all_gather(projected_part, "shard", axis=2, tiled=True)
    hidden_state = served_resid.astype(jnp.float32) + projected.astype(jnp.float32)
    mean_square = jnp.mean(hidden_state * hidden_state, axis=2, keepdims=True)
    normed = (hidden_state * lax.rsqrt(mean_square + EPSILON) * norm_gain).astype(jnp.bfloat16)
    top_count = served_ids.shape[2]
    capacity = min(tokens_here, max(2, 3 * tokens_here * top_count // (2 * experts_count)))
    flat_ids = served_ids.reshape(members, tokens_here * top_count)
    expert_hot = (
        flat_ids[:, :, None] == jnp.arange(experts_count, dtype=jnp.int32)[None, None, :]
    ).astype(jnp.int32)
    before = jnp.cumsum(expert_hot, axis=1) - expert_hot
    slot_place = jnp.sum(before * expert_hot, axis=2)
    slot_hot = (
        slot_place[:, :, None] == jnp.arange(capacity, dtype=jnp.int32)[None, None, :]
    ).astype(jnp.int32)
    place_table = (expert_hot[:, :, :, None] * slot_hot[:, :, None, :]).reshape(
        members, tokens_here, top_count, experts_count, capacity
    )
    pick_table = jnp.sum(place_table, axis=2).astype(jnp.bfloat16)
    sent_rows = jnp.einsum(
        "jtnc,jtd->njcd", pick_table, normed, preferred_element_type=jnp.float32
    ).astype(jnp.bfloat16)
    share_table = jnp.sum(
        place_table.astype(jnp.bfloat16) * served_probs[:, :, :, None, None], axis=2
    )
    partial_out = expert_rows(
        lax.all_to_all(sent_rows, "exp", split_axis=0, concat_axis=0, tiled=True),
        gate_up,
        down_proj,
    )
    expert_out = lax.psum(partial_out.astype(jnp.bfloat16), "shard")
    returned = lax.all_to_all(expert_out, "exp", split_axis=0, concat_axis=0, tiled=True)
    moe_term = jnp.einsum(
        "jtnc,njcd->jtd", share_table, returned, preferred_element_type=jnp.float32
    )
    mixed_out = (hidden_state + moe_term).astype(jnp.bfloat16)
    return mixed_out


def solution(mesh):
    return jax.shard_map(
        on_device,
        mesh=mesh,
        in_specs=(
            P("req", "exp", None),
            P("req", "exp", None),
            P("req", "exp", None),
            P("req", "exp", None),
            P(),
            P("req", None),
            P("req", None),
            P("req", ("exp", "shard"), None, None),
            P("req", ("exp", "shard"), None, None),
            P(),
            P("shard", None),
            P("exp", None, "shard", None),
            P("exp", "shard", None),
        ),
        out_specs=P("req", "exp", None),
        check_vma=False,
    )
```

profile of v0, /device:TPU:1, one launch (start us, length us, event | category | flops | bytes accessed | tf_op | source)
XLA Modules:
  0.0 1259.9 jit_solution(11993732823770950947)
XLA Ops:
  7.4 11.4 all_gather.19
  20.2 8.2 all_gather.22
  32.6 2.8 reshape_squeeze.6
  36.9 10.4 all_gather.18
  47.8 18.5 %all-gather.2.cloned.1.call-done = bf16[2,128,2304]{2,1,0:T(8,128)(2,1)} async-done(((bf16[2,16,2304]{2,1,0:T(8,128)(2,1)}), bf16[2,128,2304]{2,1,0:T(8,128)(2,1)}) %all-gather.2.cloned.1.call-update) | async-done | bytes 1179664 | tf_op jit(solution)/shard_map/all_gather | solution.py:58
  66.3 1.9 gather_fusion
  68.2 1.4 copy.90
  69.6 3.8 fusion.3
  73.6 490.0 %pmax.7 = f32[2,36,128]{2,1,0:T(8,128)S(1)} all-reduce(f32[2,36,128]{2,1,0:T(8,128)S(1)} %copy.92), channel_id=1, replica_groups=mesh['req'=4,'exp'=8,'shard'=16] {'exp','shard'}, use_global_device_ids=true, to_apply=%region_7.9 | all-reduce | flops 9216 | bytes 73728 | tf_op jit(solution)/shard_map/pmax | solution.py:96
  564.2 3.7 fusion.32
  567.9 3.1 copy.94
  571.0 3.7 select_reduce_fusion
  576.4 2.4 convert_reduce_fusion
  578.9 491.2 %psum.22 = f32[2,36,128]{2,0,1:T(2,128)S(1)} all-reduce(f32[2,36,128]{2,0,1:T(2,128)S(1)} %select_reduce_fusion.1), channel_id=1, replica_groups=mesh['req'=4,'exp'=8,'shard'=16] {'exp','shard'}, use_global_device_ids=true, to_apply=%region_12.14 | all-reduce | flops 9216 | bytes 73728 | tf_op jit(solution)/shard_map/psum | solution.py:108
  1070.8 1.5 convolution_convert_fusion.2
  1072.4 23.8 %all_gather.21 = bf16[2,16,2304]{1,0,2:T(2,128)(2,1)S(1)} all-gather(bf16[2,16,144]{1,0,2:T(2,128)(2,1)S(1)} %copy.96), channel_id=1, replica_groups=mesh['req'=4,'exp'=8,'shard'=16] {'shard'}, dimensions={2}, use_global_device_ids=true | all-gather | bytes 156672 | tf_op jit(solution)/shard_map/all_gather | solution.py:120
  1096.3 1.4 copy.97
  1098.6 20.1 %all_to_all.10 = bf16[8,2,6,2304]{3,1,2,0:T(2,128)(2,1)S(1)} all-to-all(bf16[8,2,6,2304]{3,1,2,0:T(2,128)(2,1)S(1)} %copy.100), channel_id=1, replica_groups=mesh['req'=4,'exp'=8,'shard'=16] {'exp'}, dimensions={0} | all-to-all | bytes 884736 | tf_op jit(solution)/shard_map/all_to_all | solution.py:146
  1119.6 1.6 fusion.4
  1122.5 105.0 %all-reduce.5.cloned.1.call-done = bf16[8,2,6,2304]{3,0,2,1:T(8,128)(2,1)} async-done(((bf16[8,2,6,2304]{3,0,2,1:T(8,128)(2,1)}), bf16[8,2,6,2304]{3,0,2,1:T(8,128)(2,1)}) %all-reduce.5.cloned.1.call-update) | async-done | bytes 442384 | tf_op jit(solution)/shard_map/psum | solution.py:150
  1227.5 2.1 copy.105
  1229.6 6.7 all-to-all-start.1
  1236.3 7.9 all_gather.23
  1244.9 7.6 all-to-all-done.1
  (83 shorter events, 16.3 us)
Async XLA Ops:
  6.5 1113.1 %copy-start = (bf16[1,2,180,2304]{3,1,2,0:T(2,128)(2,1)S(1)}, bf16[1,2,180,2304]{3,1,2,0:T(2,128)(2,1)}, u32[]{:S(2)}) copy-start(bf16[1,2,180,2304]{3,1,2,0:T(2,128)(2,1)} %param.26) | copy-start | bytes 4976644
  6.5 28.8 %copy-start.3 = (bf16[1,2,64,2304]{3,2,1,0:T(8,128)(2,1)S(1)}, bf16[1,2,64,2304]{3,2,1,0:T(8,128)(2,1)}, u32[]{:S(2)}) copy-start(bf16[1,2,64,2304]{3,2,1,0:T(8,128)(2,1)} %param.23) | copy-start | bytes 1769476
  6.5 59.7 %all-gather.2.cloned.1.call-start = ((), (), s32[]{:S(2)}) async-start(), calls=%async_computation.2 | async-start | bytes 1327104 | tf_op jit(solution)/shard_map/all_gather | solution.py:58
  18.9 17.9 %copy-start.8 = (s32[1,2]{1,0:T(1,128)S(1)}, s32[1,2]{1,0:T(1,128)}, u32[]{:S(2)}) copy-start(s32[1,2]{1,0:T(1,128)} %param.20) | copy-start | bytes 28
  19.4 17.5 %copy-start.4 = (bf16[2,16,2304]{2,1,0:T(8,128)(2,1)S(1)}, bf16[2,16,2304]{2,1,0:T(8,128)(2,1)}, u32[]{:S(2)}) copy-start(bf16[2,16,2304]{2,1,0:T(8,128)(2,1)} %param.16) | copy-start | bytes 442372
  20.2 1050.6 %all-reduce.3.cloned.1.call-start = ((), (), s32[]{:S(2)}) async-start(), calls=%async_computation.3 | async-start | bytes 4718592 | tf_op jit(solution)/shard_map/psum | solution.py:108
  69.6 494.6 %copy-start.1 = (bf16[1,2,64,2304]{2,3,1,0:T(8,128)(2,1)S(1)}, bf16[1,2,64,2304]{2,3,1,0:T(8,128)(2,1)}, u32[]{:S(2)}) copy-start(bf16[1,2,64,2304]{2,3,1,0:T(8,128)(2,1)} %copy.110) | copy-start | bytes 1769476
  574.7 0.8 copy-start.5
  574.7 652.8 %all-reduce.5.cloned.1.call-start = ((), (), s32[]{:S(2)}) async-start(), calls=%async_computation.4 | async-start | bytes 884736 | tf_op jit(solution)/shard_map/psum | solution.py:150
  1070.7 27.2 %copy-start.6 = (f32[2304]{0:T(1024)S(1)}, f32[2304]{0:T(1024)}, u32[]{:S(2)}) copy-start(f32[2304]{0:T(1024)} %param.24) | copy-start | bytes 27652
  1118.7 2.8 copy-start.2
  1121.3 115.0 %copy-start.7 = (bf16[2,16,2]{1,2,0:T(2,128)(2,1)S(1)}, bf16[2,16,2]{1,2,0:T(2,128)(2,1)}, u32[]{:S(2)}) copy-start(bf16[2,16,2]{1,2,0:T(2,128)(2,1)} %param.18) | copy-start | bytes 388
  1229.6 22.9 %all-to-all-start.1 = ((bf16[8,2,6,2304]{3,1,2,0:T(2,128)(2,1)}), bf16[8,2,6,2304]{3,1,2,0:T(2,128)(2,1)S(1)}, u32[]{:S(2)}, u32[]{:S(2)}) async-start(bf16[8,2,6,2304]{3,1,2,0:T(2,128)(2,1)} %copy.105), calls=%async_computation.1 | async-start | bytes 884736 | tf_op jit(solution)/shard_map/all_to_all | solution.py:151
Sparse Core Ops, SparseCore 0:
  20.3 45.9 all-gather.1
  574.8 197.8 all-reduce.2
  1122.6 104.7 all-reduce.4
where the time goes:
time: 1260 us
  blocking collectives  1060 us (84%)
  waiting for transfers between devices  131 us (10%)
  local copies, waits for them, and re-layouts  20.2 us (2%)
  between operations  13.4 us (1%)
  matrix products  12.9 us (1%)
    psum x1, blocking collectives, on_device(): context_all, totals_all = lax.psum((context, totals), ('exp', 'shard'))  491 us
    pmax x1, blocking collectives, on_device(): row_peak = lax.pmax(local_peak, ('exp', 'shard'))  490 us
    psum x1, waiting for transfers between devices, on_device(): expert_out = lax.psum(partial_out.astype(jnp.bfloat16), 'shard')  105 us
  transfers between devices with their start and end apart: 4, of which 3 were waited for; matrix products, arithmetic and copies ran while one was open for 1% of the time, Pallas kernels for 0%

commit v1 on v0

--- a/solution.py
+++ b/solution.py
@@ -105,7 +105,9 @@
     page_context = page_context.reshape(pages_here, stretch_len, width)
     context = jnp.sum(jnp.where(owner_hot[:, :, None, None], page_context[:, None], 0.0), axis=0)
     totals = jnp.sum(jnp.where(owner_hot[:, :, None, None], page_totals[:, None], 0.0), axis=0)
-    context_all, totals_all = lax.psum((context, totals), ("exp", "shard"))
+    context_all, totals_all = jax.lax.psum(
+        jax.lax.psum((context, totals), axis_name="shard"), "exp"
+    )
     context_mine = lax.dynamic_slice_in_dim(context_all, exp_index * tokens_here, tokens_here, 1)
     totals_mine = lax.dynamic_slice_in_dim(totals_all, exp_index * tokens_here, tokens_here, 2)
     per_head = context_mine.reshape(members, tokens_here, H, head_size)

time: 1260 us -> 989 us (0.78)
  blocking collectives: 1060 us -> 651 us
  waiting for transfers between devices: 131 us -> 274 us
    psum x1 -> x2, blocking collectives: 491 us -> 75.3 us  [the longest x1 50 us: on_device(): jax.lax.psum((context, totals), axis_name='shard')]
    psum x1 -> x2, waiting for transfers between devices: 0.02 us -> 119 us  [the longest x1 119 us: on_device(): jax.lax.psum((context, totals), axis_name='shard')]
    all_gather x1, waiting for transfers between devices: 18.5 us -> 39.5 us  [on_device(): group_query = lax.all_gather(served_query, 'exp', axis=1, tiled=True)]
  transfers between devices with their start and end apart: 4 -> 5, of which waited for: 3 -> 4; matrix products, arithmetic and copies ran while one was open for 1% -> 1% of each run, Pallas kernels for 0% -> 0%
where the time goes in v1:
time: 989 us
  blocking collectives  651 us (66%)
  waiting for transfers between devices  274 us (28%)
  local copies, waits for them, and re-layouts  19.4 us (2%)
  between operations  13.4 us (1%)
  matrix products  13 us (1%)
  other arithmetic  11.3 us (1%)
    pmax x1, blocking collectives, on_device(): row_peak = lax.pmax(local_peak, ('exp', 'shard'))  490 us
    psum x1, waiting for transfers between devices, on_device(): jax.lax.psum((context, totals), axis_name='shard')  119 us
    psum x1, waiting for transfers between devices, on_device(): expert_out = lax.psum(partial_out.astype(jnp.bfloat16), 'shard')  107 us
    psum x1, blocking collectives, on_device(): jax.lax.psum((context, totals), axis_name='shard')  50 us
    all_gather x1, waiting for transfers between devices, on_device(): group_query = lax.all_gather(served_query, 'exp', axis=1, tiled=True)  39.5 us
    all_gather x1, blocking collectives, on_device(): projected = lax.all_gather(projected_part, 'shard', axis=2, tiled=True)  27.8 us
    psum x1, blocking collectives, on_device(): jax.lax.psum(jax.lax.psum((context, totals), axis_name='shard'), 'exp')  25.3 us
    all_to_all x1, blocking collectives, on_device(): lax.all_to_all(sent_rows, 'exp', split_axis=0, concat_axis=0, tiled=True)  20.3 us
  transfers between devices with their start and end apart: 5, of which 4 were waited for; matrix products, arithmetic and copies ran while one was open for 1% of the time, Pallas kernels for 0%

profile of v1, /device:TPU:1, one launch (start us, length us, event | category | flops | bytes accessed | tf_op | source)
XLA Modules:
  0.0 988.5 jit_solution(4497270542862573643)
XLA Ops:
  7.4 11.4 %all_gather.19 = bf16[8,16,2304]{2,1,0:T(8,128)(2,1)S(1)} all-gather(bf16[2,16,2304]{2,1,0:T(8,128)(2,1)} %param.15), channel_id=1, replica_groups=mesh['req'=4,'exp'=8,'shard'=16] {'req'}, dimensions={0}, use_global_device_ids=true | all-gather | bytes 737280 | tf_op jit(solution)/shard_map/all_gather | solution.py:48
  22.1 2.8 reshape_squeeze.6
  26.8 39.5 %all-gather.2.cloned.1.call-done = bf16[2,128,2304]{2,1,0:T(8,128)(2,1)} async-done(((bf16[2,16,2304]{2,1,0:T(8,128)(2,1)}), bf16[2,128,2304]{2,1,0:T(8,128)(2,1)}) %all-gather.2.cloned.1.call-update) | async-done | bytes 1179664 | tf_op jit(solution)/shard_map/all_gather | solution.py:58
  66.3 1.9 gather_fusion
  69.6 3.8 fusion.3
  73.6 489.8 %pmax.7 = f32[2,36,128]{2,1,0:T(8,128)S(1)} all-reduce(f32[2,36,128]{2,1,0:T(8,128)S(1)} %copy.92), channel_id=1, replica_groups=mesh['req'=4,'exp'=8,'shard'=16] {'exp','shard'}, use_global_device_ids=true, to_apply=%region_7.9 | all-reduce | flops 9216 | bytes 73728 | tf_op jit(solution)/shard_map/pmax | solution.py:96
  564.1 3.7 fusion.32
  567.8 3.0 copy.94
  570.8 3.8 select_reduce_fusion
  574.7 119.4 %all-reduce.4.cloned.1.call-done = f32[2,128,2304]{2,1,0:T(8,128)} async-done(((f32[2,128,2304]{2,1,0:T(8,128)}), f32[2,128,2304]{2,1,0:T(8,128)}) %all-reduce.4.cloned.1.call-update) | async-done | bytes 2359312 | tf_op jit(solution)/shard_map/psum | solution.py:109
  694.2 8.4 all_gather.22
  703.9 10.0 %all_gather.18 = bf16[8,16,2304]{2,1,0:T(8,128)(2,1)S(1)} all-gather(bf16[2,16,2304]{2,1,0:T(8,128)(2,1)S(1)} %copy-done.4), channel_id=1, replica_groups=mesh['req'=4,'exp'=8,'shard'=16] {'req'}, dimensions={0}, use_global_device_ids=true | all-gather | bytes 737280 | tf_op jit(solution)/shard_map/all_gather | solution.py:49
  714.6 2.4 convert_reduce_fusion
  717.1 50.0 %psum.37 = f32[2,36,128]{2,0,1:T(2,128)S(1)} all-reduce(f32[2,36,128]{2,0,1:T(2,128)S(1)} %select_reduce_fusion.1), channel_id=1, replica_groups=mesh['req'=4,'exp'=8,'shard'=16] {'shard'}, use_global_device_ids=true, to_apply=%region_13.15 | all-reduce | flops 9216 | bytes 73728 | tf_op jit(solution)/shard_map/psum | solution.py:109
  767.1 25.3 %psum.38 = f32[2,36,128]{2,0,1:T(2,128)S(1)} all-reduce(f32[2,36,128]{2,0,1:T(2,128)S(1)} %psum.37), channel_id=1, replica_groups=mesh['req'=4,'exp'=8,'shard'=16] {'exp'}, use_global_device_ids=true, to_apply=%region_14.16 | all-reduce | flops 9216 | bytes 73728 | tf_op jit(solution)/shard_map/psum | solution.py:108
  793.1 1.5 convolution_convert_fusion.2
  794.8 27.8 %all_gather.21 = bf16[2,16,2304]{1,0,2:T(2,128)(2,1)S(1)} all-gather(bf16[2,16,144]{1,0,2:T(2,128)(2,1)S(1)} %copy.96), channel_id=1, replica_groups=mesh['req'=4,'exp'=8,'shard'=16] {'shard'}, dimensions={2}, use_global_device_ids=true | all-gather | bytes 156672 | tf_op jit(solution)/shard_map/all_gather | solution.py:122
  824.9 20.3 %all_to_all.10 = bf16[8,2,6,2304]{3,1,2,0:T(2,128)(2,1)S(1)} all-to-all(bf16[8,2,6,2304]{3,1,2,0:T(2,128)(2,1)S(1)} %copy.100), channel_id=1, replica_groups=mesh['req'=4,'exp'=8,'shard'=16] {'exp'}, dimensions={0} | all-to-all | bytes 884736 | tf_op jit(solution)/shard_map/all_to_all | solution.py:148
  846.2 1.6 fusion.4
  849.1 107.0 %all-reduce.8.cloned.1.call-done = bf16[8,2,6,2304]{3,0,2,1:T(8,128)(2,1)} async-done(((bf16[8,2,6,2304]{3,0,2,1:T(8,128)(2,1)}), bf16[8,2,6,2304]{3,0,2,1:T(8,128)(2,1)}) %all-reduce.8.cloned.1.call-update) | async-done | bytes 442384 | tf_op jit(solution)/shard_map/psum | solution.py:152
  956.1 2.1 copy.105
  958.2 6.7 all-to-all-start.1
  964.9 7.9 all_gather.23
  973.5 7.6 all-to-all-done.1
  (87 shorter events, 17.3 us)
Async XLA Ops:
  6.5 839.6 %copy-start = (bf16[1,2,180,2304]{3,1,2,0:T(2,128)(2,1)S(1)}, bf16[1,2,180,2304]{3,1,2,0:T(2,128)(2,1)}, u32[]{:S(2)}) copy-start(bf16[1,2,180,2304]{3,1,2,0:T(2,128)(2,1)} %param.26) | copy-start | bytes 4976644
  6.5 18.4 %copy-start.3 = (bf16[1,2,64,2304]{3,2,1,0:T(8,128)(2,1)S(1)}, bf16[1,2,64,2304]{3,2,1,0:T(8,128)(2,1)}, u32[]{:S(2)}) copy-start(bf16[1,2,64,2304]{3,2,1,0:T(8,128)(2,1)} %param.23) | copy-start | bytes 1769476
  6.5 59.8 %all-gather.2.cloned.1.call-start = ((), (), s32[]{:S(2)}) async-start(), calls=%async_computation.2 | async-start | bytes 1327104 | tf_op jit(solution)/shard_map/all_gather | solution.py:58
  18.9 7.5 copy-start.8
  20.2 673.9 %all-reduce.4.cloned.1.call-start = ((), (), s32[]{:S(2)}) async-start(), calls=%async_computation.3 | async-start | bytes 4718592 | tf_op jit(solution)/shard_map/psum | solution.py:109
  69.6 494.4 %copy-start.1 = (bf16[1,2,64,2304]{2,3,1,0:T(8,128)(2,1)S(1)}, bf16[1,2,64,2304]{2,3,1,0:T(8,128)(2,1)}, u32[]{:S(2)}) copy-start(bf16[1,2,64,2304]{2,3,1,0:T(8,128)(2,1)} %copy.110) | copy-start | bytes 1769476
  574.6 119.6 %copy-start.6 = (s32[2,16,2]{1,2,0:T(2,128)S(1)}, s32[2,16,2]{1,2,0:T(2,128)}, u32[]{:S(2)}) copy-start(s32[2,16,2]{1,2,0:T(2,128)} %param.17) | copy-start | bytes 772
  574.6 129.3 %copy-start.4 = (bf16[2,16,2304]{2,1,0:T(8,128)(2,1)S(1)}, bf16[2,16,2304]{2,1,0:T(8,128)(2,1)}, u32[]{:S(2)}) copy-start(bf16[2,16,2304]{2,1,0:T(8,128)(2,1)} %param.16) | copy-start | bytes 442372
  574.6 218.5 %all-reduce.6.cloned.1.call-start = ((), (), s32[]{:S(2)}) async-start(), calls=%async_computation.4 | async-start | bytes 4718592 | tf_op jit(solution)/shard_map/psum | solution.py:108
  694.1 261.9 %all-reduce.8.cloned.1.call-start = ((), (), s32[]{:S(2)}) async-start(), calls=%async_computation.5 | async-start | bytes 884736 | tf_op jit(solution)/shard_map/psum | solution.py:152
  793.0 31.1 %copy-start.5 = (f32[2304]{0:T(1024)S(1)}, f32[2304]{0:T(1024)}, u32[]{:S(2)}) copy-start(f32[2304]{0:T(1024)} %param.24) | copy-start | bytes 27652
  845.2 2.8 copy-start.2
  847.8 117.1 %copy-start.7 = (bf16[2,16,2]{1,2,0:T(2,128)(2,1)S(1)}, bf16[2,16,2]{1,2,0:T(2,128)(2,1)}, u32[]{:S(2)}) copy-start(bf16[2,16,2]{1,2,0:T(2,128)(2,1)} %param.18) | copy-start | bytes 388
  958.2 22.9 %all-to-all-start.1 = ((bf16[8,2,6,2304]{3,1,2,0:T(2,128)(2,1)}), bf16[8,2,6,2304]{3,1,2,0:T(2,128)(2,1)S(1)}, u32[]{:S(2)}, u32[]{:S(2)}) async-start(bf16[8,2,6,2304]{3,1,2,0:T(2,128)(2,1)} %copy.105), calls=%async_computation.1 | async-start | bytes 884736 | tf_op jit(solution)/shard_map/all_to_all | solution.py:153
Sparse Core Ops, SparseCore 0:
  20.3 45.9 all-gather.1
  574.8 119.3 all-reduce.3
  696.5 87.6 all-reduce.5
  849.2 106.8 all-reduce.7
